TPU v7x, 32 devices: a whole 2x2x4 slice. The times are simulated.
32 devices in a mesh: row: 8 (over y, x, core), col: 4 (over z).
Axes of the slice: x: 2, y: 2, z: 4, core: 2. Of those that a mesh axis runs over, the one named last changes fastest.
Arguments:
- tokens: bfloat16 [192, 8192], P('col', 'row'), may hold values from -6 to 6
- grad_out: bfloat16 [192, 8192], P('col', 'row'), may hold values from -6 to 6
- gate_weight: bfloat16 [8192, 14336], P('row', 'col'), may hold values from -0.0625 to 0.0625
- up_weight: bfloat16 [8192, 14336], P('row', 'col'), may hold values from -0.0625 to 0.0625
- down_weight: bfloat16 [14336, 8192], P('col', 'row'), may hold values from -0.046875 to 0.046875
Outputs:
- grad_tokens: bfloat16 [192, 8192], P('col', 'row')
- grad_gate_weight: bfloat16 [8192, 14336], P('row', 'col')
- grad_up_weight: bfloat16 [8192, 14336], P('row', 'col')
- grad_down_weight: bfloat16 [14336, 8192], P('col', 'row')
All inputs are finite; a program needn't handle non-finite values.
Results may differ from a plain program's by a relative error of at most 0.024.
Values may be sent and summed in bfloat16 or wider, within the bound.
No kernel may reach another device: no remote copies, remote signals or barrier semaphores. Data moves between devices by JAX's collectives and lax.ppermute only.
A program may use at most 128 MiB of HBM per device.

v0:
```python
import jax
import jax.numpy as jnp
from jax import lax
from jax.sharding import PartitionSpec as P


def contract_first(left, right):
    return lax.dot_general(
        left, right, (((0,), (0,)), ((), ())), preferred_element_type=jnp.float32
    )


def contract_last(left, right):
    return lax.dot_general(
        left, right, (((1,), (1,)), ((), ())), preferred_element_type=jnp.float32
    )


def gated_grads(gate_sum, up_sum, grad_hidden):
    sigmoid_gate = jax.nn.sigmoid(gate_sum)
    hidden = (gate_sum * sigmoid_gate * up_sum).astype(jnp.bfloat16)
    grad_up = (grad_hidden * gate_sum * sigmoid_gate).astype(jnp.bfloat16)
    grad_gate = (
        grad_hidden * up_sum * sigmoid_gate * (1.0 + gate_sum * (1.0 - sigmoid_gate))
    ).astype(jnp.bfloat16)
    return (hidden, grad_gate, grad_up)


def pick_chunks(units, wanted):
    for n in range(wanted, 0, -1):
        if units % n == 0 and units // n % 128 == 0:
            return n
    return 1


N_CHUNKS = 2


def body(tokens, grad_out, gate_weight, up_weight, down_weight):
    feat = tokens.shape[1]
    both = jnp.concatenate([tokens, grad_out], axis=1)
    both_all = lax.all_gather(both, "col", axis=0, tiled=True)
    tok_all = both_all[:, :feat]
    grad_all = both_all[:, feat:]
    tok_t = tok_all.T
    units = gate_weight.shape[1]
    n_chunks = pick_chunks(units, N_CHUNKS)
    span = units // n_chunks
    acc_gate, acc_up, acc_down = ([], [], [])
    partial_grad = None
    prev = None
    for k in range(n_chunks):
        lo = k * span
        gw = gate_weight[:, lo : lo + span]
        uw = up_weight[:, lo : lo + span]
        dw = down_weight[lo : lo + span, :]
        parts = (
            jnp.dot(tok_all, gw, preferred_element_type=jnp.float32).astype(jnp.bfloat16),
            jnp.dot(tok_all, uw, preferred_element_type=jnp.float32).astype(jnp.bfloat16),
            contract_last(grad_all, dw).astype(jnp.bfloat16),
        )
        if prev is not None:
            parts, _ = lax.optimization_barrier((parts, prev))
        sums = lax.psum(parts, "row")
        prev = sums
        gate_sum, up_sum, grad_hidden = (s.astype(jnp.float32) for s in sums)
        hidden, grad_gate, grad_up = gated_grads(gate_sum, up_sum, grad_hidden)
        acc_gate.append(
            jnp.dot(tok_t, grad_gate, preferred_element_type=jnp.float32).astype(jnp.bfloat16)
        )
        acc_up.append(
            jnp.dot(tok_t, grad_up, preferred_element_type=jnp.float32).astype(jnp.bfloat16)
        )
        acc_down.append(contract_first(hidden, grad_all).astype(jnp.bfloat16))
        part = contract_last(grad_gate, gw) + contract_last(grad_up, uw)
        partial_grad = part if partial_grad is None else partial_grad + part
    grad_tokens = lax.psum_scatter(
        partial_grad.astype(jnp.bfloat16), "col", scatter_dimension=0, tiled=True
    )
    return (
        grad_tokens,
        jnp.concatenate(acc_gate, axis=1),
        jnp.concatenate(acc_up, axis=1),
        jnp.concatenate(acc_down, axis=0),
    )


def solution(mesh):
    return jax.shard_map(
        body,
        mesh=mesh,
        in_specs=(
            P("col", "row"),
            P("col", "row"),
            P("row", "col"),
            P("row", "col"),
            P("col", "row"),
        ),
        out_specs=(P("col", "row"), P("row", "col"), P("row", "col"), P("col", "row")),
        check_vma=False,
    )
```

profile of v0, /device:TPU:0, one launch (start us, length us, event | category | flops | bytes accessed | tf_op | source)
XLA Modules:
  0.0 214.4 jit_solution(11317851768424443296)
XLA Ops:
  7.2 0.0 all-reduce.7.cloned.1.call-start
  7.2 1.0 pad_maximum_fusion.3
  8.2 0.0 slice-start
  8.2 21.4 %all_gather.3 = bf16[192,2048]{1,0:T(8,128)(2,1)S(1)} all-gather(bf16[48,2048]{1,0:T(8,128)(2,1)S(1)} %pad_maximum_fusion.3), channel_id=1, replica_groups=mesh['row'=8,'col'=4] {'col'}, dimensions={0}, use_global_device_ids=true | all-gather | bytes 983040 | tf_op jit(solution)/shard_map/all_gather | solution.py:42
  29.6 0.0 slice-start.1
  29.6 3.9 %fusion.23 = bf16[192,1792]{1,0:T(8,128)(2,1)} fusion(bf16[1024,3584]{1,0:T(8,128)(2,1)} %param.7, bf16[192,2048]{1,0:T(8,128)(2,1)S(1)} %all_gather.3), kind=kOutput, calls=%fused_computation.30 | convolution fusion | flops 704987136 | bytes 4751360 | tf_op jit(solution)/shard_map/dot_general | solution.py:58
  33.5 3.8 %fusion.20 = bf16[192,1792]{1,0:T(8,128)(2,1)} fusion(bf16[1024,3584]{1,0:T(8,128)(2,1)} %param.8, bf16[192,2048]{1,0:T(8,128)(2,1)S(1)} %all_gather.3), kind=kOutput, calls=%fused_computation.29 | convolution fusion | flops 704987136 | bytes 4751360 | tf_op jit(solution)/shard_map/dot_general | solution.py:59
  37.3 0.0 slice-done
  37.3 0.0 slice-done.1
  37.3 2.2 %fusion.32 = bf16[192,1792]{1,0:T(8,128)(2,1)} fusion(bf16[3584,1024]{1,0:T(8,128)(2,1)S(1)} %bitcast.1, bf16[192,2048]{1,0:T(8,128)(2,1)S(1)} %all_gather.3), kind=kOutput, calls=%fused_computation.33 | convolution fusion | flops 704987136 | bytes 4751360 | tf_op jit(solution)/shard_map/dot_general | solution.py:14
  39.6 0.0 all-reduce.7.cloned.1.call-update
  39.6 0.0 all-reduce.5.cloned.1.call-start
  39.6 3.8 %fusion.26 = bf16[192,1792]{1,0:T(8,128)(2,1)} fusion(bf16[1024,3584]{1,0:T(8,128)(2,1)} %param.7, bf16[192,2048]{1,0:T(8,128)(2,1)S(1)} %all_gather.3), kind=kOutput, calls=%fused_computation.31 | convolution fusion | flops 704987136 | bytes 4751360 | tf_op jit(solution)/shard_map/dot_general | solution.py:58
  43.4 4.2 %fusion.29 = bf16[192,1792]{1,0:T(8,128)(2,1)} fusion(bf16[1024,3584]{1,0:T(8,128)(2,1)} %param.8, bf16[192,2048]{1,0:T(8,128)(2,1)S(1)} %all_gather.3), kind=kOutput, calls=%fused_computation.32 | convolution fusion | flops 704987136 | bytes 4751360 | tf_op jit(solution)/shard_map/dot_general | solution.py:59
  47.6 4.3 %fusion.35 = bf16[192,1792]{1,0:T(8,128)(2,1)} fusion(bf16[3584,1024]{1,0:T(8,128)(2,1)} %param.9, bf16[192,2048]{1,0:T(8,128)(2,1)S(1)} %all_gather.3), kind=kOutput, calls=%fused_computation.34 | convolution fusion | flops 704987136 | bytes 4751360 | tf_op jit(solution)/shard_map/dot_general | solution.py:14
  51.9 49.2 %all-reduce.7.cloned.1.call-done = (bf16[192,1792]{1,0:T(8,128)(2,1)}, bf16[192,1792]{1,0:T(8,128)(2,1)}, bf16[192,1792]{1,0:T(8,128)(2,1)}) async-done(((bf16[192,1792]{1,0:T(8,128)(2,1)}, bf16[192,1792]{1,0:T(8,128)(2,1)}, bf16[192,1792]{1,0:T(8,128)(2,1)}), (bf16[192,1792]{1,0:T(8,128)(2,1)}, bf16[192,1792]{1,0:T(8,128)(2,1)}, bf16[192,1792]{1,0:T(8,128)(2,1)})) %all-reduce.7.cloned.1.call-update) | async-done | bytes 2064400 | tf_op jit(solution)/shard_map/psum | solution.py:64
  101.1 0.0 copy-start.1
  101.1 4.5 %convolution_convert_fusion.1 = bf16[1792,1024]{1,0:T(8,128)(2,1)} fusion(bf16[192,1792]{1,0:T(8,128)(2,1)} %get-tuple-element.14, bf16[192,1792]{1,0:T(8,128)(2,1)} %get-tuple-element.13, bf16[192,2048]{1,0:T(8,128)(2,1)S(1)} %all_gather.3), kind=kOutput, calls=%fused_computation.4 | convolution fusion | flops 709230592 | bytes 5439488 | tf_op jit(solution)/shard_map/dot_general | solution.py:8
  105.6 0.0 copy-done.1
  105.6 0.0 copy-done.2
  105.6 0.0 copy-done.3
  105.6 3.2 %convolution_convert_fusion.5 = bf16[1024,1792]{1,0:T(8,128)(2,1)} fusion(bf16[192,2048]{1,0:T(8,128)(2,1)S(1)} %all_gather.3, bf16[192,1792]{1,0:T(8,128)(2,1)S(1)} %copy-done.3, bf16[192,1792]{1,0:T(8,128)(2,1)S(1)} %copy-done.2, bf16[192,1792]{1,0:T(8,128)(2,1)S(1)} %copy-done.1), kind=kOutput, calls=%fused_computation.8 | convolution fusion | flops 710950912 | bytes 6127616 | tf_op jit(solution)/shard_map/dot_general | solution.py:69
  108.7 0.0 all-reduce.5.cloned.1.call-update
  108.8 0.2 reduce-scatter.2.cloned.1.call-start
  109.0 3.0 %convolution_convert_fusion.3 = bf16[1024,1792]{1,0:T(8,128)(2,1)} fusion(bf16[192,2048]{1,0:T(8,128)(2,1)S(1)} %all_gather.3, bf16[192,1792]{1,0:T(8,128)(2,1)S(1)} %copy-done.1, bf16[192,1792]{1,0:T(8,128)(2,1)S(1)} %copy-done.2), kind=kOutput, calls=%fused_computation.6 | convolution fusion | flops 709230592 | bytes 5439488 | tf_op jit(solution)/shard_map/dot_general | solution.py:72
  112.0 4.6 %fusion.12 = f32[192,1024]{1,0:T(8,128)} fusion(bf16[1024,3584]{1,0:T(8,128)(2,1)} %param.7, bf16[192,1792]{1,0:T(8,128)(2,1)S(1)} %copy-done.3, bf16[192,1792]{1,0:T(8,128)(2,1)S(1)} %copy-done.2, bf16[192,1792]{1,0:T(8,128)(2,1)S(1)} %copy-done.1), kind=kOutput, calls=%fused_computation.21 | convolution fusion | flops 709115904 | bytes 6520832 | tf_op jit(solution)/shard_map/dot_general | solution.py:14
  116.6 53.7 %all-reduce.5.cloned.1.call-done = (bf16[192,1792]{1,0:T(8,128)(2,1)}, bf16[192,1792]{1,0:T(8,128)(2,1)}, bf16[192,1792]{1,0:T(8,128)(2,1)}) async-done(((bf16[192,1792]{1,0:T(8,128)(2,1)}, bf16[192,1792]{1,0:T(8,128)(2,1)}, bf16[192,1792]{1,0:T(8,128)(2,1)}), (bf16[192,1792]{1,0:T(8,128)(2,1)}, bf16[192,1792]{1,0:T(8,128)(2,1)}, bf16[192,1792]{1,0:T(8,128)(2,1)})) %all-reduce.5.cloned.1.call-update) | async-done | bytes 2064400 | tf_op jit(solution)/shard_map/psum | solution.py:64
  170.3 3.9 %fusion.4 = f32[192,1024]{1,0:T(8,128)S(1)} fusion(bf16[1024,3584]{1,0:T(8,128)(2,1)} %param.8, bf16[192,1792]{1,0:T(8,128)(2,1)} %get-tuple-element.10, bf16[192,1792]{1,0:T(8,128)(2,1)} %get-tuple-element.11), kind=kOutput, calls=%fused_computation.13 | convolution fusion | flops 707395584 | bytes 5832704 | tf_op jit(solution)/shard_map/dot_general | solution.py:14
  174.2 0.0 copy-done.4
  174.2 0.0 copy-done.5
  174.2 0.0 copy-start.6
  174.2 3.1 %convolution_convert_fusion.2 = bf16[1024,1792]{1,0:T(8,128)(2,1)} fusion(bf16[192,2048]{1,0:T(8,128)(2,1)S(1)} %all_gather.3, bf16[192,1792]{1,0:T(8,128)(2,1)S(1)} %copy-done.4, bf16[192,1792]{1,0:T(8,128)(2,1)S(1)} %copy-done.5), kind=kOutput, calls=%fused_computation.5 | convolution fusion | flops 709230592 | bytes 5439488 | tf_op jit(solution)/shard_map/dot_general | solution.py:72
  177.4 0.0 copy-done.6
  177.4 3.2 %convolution_convert_fusion.4 = bf16[1024,1792]{1,0:T(8,128)(2,1)} fusion(bf16[192,2048]{1,0:T(8,128)(2,1)S(1)} %all_gather.3, bf16[192,1792]{1,0:T(8,128)(2,1)S(1)} %copy-done.6, bf16[192,1792]{1,0:T(8,128)(2,1)S(1)} %copy-done.5, bf16[192,1792]{1,0:T(8,128)(2,1)S(1)} %copy-done.4), kind=kOutput, calls=%fused_computation.7 | convolution fusion | flops 710950912 | bytes 6127616 | tf_op jit(solution)/shard_map/dot_general | solution.py:69
  180.6 3.1 %convolution_convert_fusion = bf16[1792,1024]{1,0:T(8,128)(2,1)} fusion(bf16[192,1792]{1,0:T(8,128)(2,1)S(1)} %copy-done.6, bf16[192,1792]{1,0:T(8,128)(2,1)S(1)} %copy-done.4, bf16[192,2048]{1,0:T(8,128)(2,1)S(1)} %all_gather.3), kind=kOutput, calls=%fused_computation.3 | convolution fusion | flops 709230592 | bytes 5439488 | tf_op jit(solution)/shard_map/dot_general | solution.py:8
  183.7 0.0 slice-done.2
  183.7 0.0 slice-done.3
  183.7 1.4 fusion.64
  185.1 0.0 slice-done.4
  185.1 0.3 slice-done.5
  185.4 0.0 copy-done.7
  185.4 2.2 %fusion.67 = bf16[192,1024]{1,0:T(8,128)(2,1)} fusion(f32[192,1024]{1,0:T(8,128)S(1)} %fusion.64, f32[192,1024]{1,0:T(8,128)S(1)} %copy-done.7, bf16[1024,3584]{1,0:T(8,128)(2,1)S(1)} %bitcast.5, bf16[192,1792]{1,0:T(8,128)(2,1)S(1)} %copy-done.1, bf16[192,1792]{1,0:T(8,128)(2,1)S(1)} %copy-done.2), kind=kOutput, calls=%fused_computation.70 | convolution fusion | flops 707985408 | bytes 7012352 | tf_op jit(solution)/shard_map/dot_general | solution.py:14
  187.6 0.0 reduce-scatter.2.cloned.1.call-update
  187.6 0.0 copy-start
  187.6 7.2 %pad_maximum_fusion.2 = bf16[3584,1024]{1,0:T(8,128)(2,1)} fusion(bf16[1792,1024]{1,0:T(8,128)(2,1)} %convolution_convert_fusion, bf16[1792,1024]{1,0:T(8,128)(2,1)} %convolution_convert_fusion.1), kind=kLoop, calls=%fused_computation.2 | loop fusion | flops 14680064 | bytes 14680064 | tf_op jit(solution)/shard_map/concatenate | solution.py:84
  194.8 0.0 copy-done
  194.8 9.4 %pad_maximum_fusion = (bf16[1024,3584]{1,0:T(8,128)(2,1)}, bf16[1024,3584]{1,0:T(8,128)(2,1)}) fusion(bf16[1024,1792]{1,0:T(8,128)(2,1)} %convolution_convert_fusion.4, bf16[1024,1792]{1,0:T(8,128)(2,1)S(1)} %copy-done, bf16[1024,1792]{1,0:T(8,128)(2,1)} %convolution_convert_fusion.2, bf16[1024,1792]{1,0:T(8,128)(2,1)} %convolution_convert_fusion.3), kind=kLoop, calls=%fused_computation | loop fusion | flops 29360128 | bytes 29360128 | tf_op jit(solution)/shard_map/concatenate | solution.py:82
  204.3 3.6 %reduce-scatter.2.cloned.1.call-done = bf16[48,1024]{1,0:T(8,128)(2,1)} async-done(((bf16[192,1024]{1,0:T(8,128)(2,1)}), bf16[48,1024]{1,0:T(8,128)(2,1)}) %reduce-scatter.2.cloned.1.call-update) | async-done | bytes 98320 | tf_op jit(solution)/shard_map/reduce_scatter | solution.py:77
  (12 shorter events, 0.0 us)
Async XLA Ops:
  7.2 94.0 %all-reduce.7.cloned.1.call-start = ((), (), s32[]{:S(2)}) async-start(), calls=%async_computation.3 | async-start | bytes 4128768 | tf_op jit(solution)/shard_map/psum | solution.py:64
  8.2 29.2 %slice-start = ((s8[7340032]{0:T(1024)(128)(4,1)}), s8[4194304]{0:T(1024)(128)(4,1)S(1)}, s32[]{:S(2)}) async-start(s8[7340032]{0:T(1024)(128)(4,1)} %bitcast), calls=%async_computation.4 | async-start | bytes 8388608
  29.6 7.7 %slice-start.1 = ((s8[7340032]{0:T(1024)(128)(4,1)}), s8[3145728]{0:T(1024)(128)(4,1)S(1)}, s32[]{:S(2)}) async-start(s8[7340032]{0:T(1024)(128)(4,1)} %bitcast), calls=%async_computation.5 | async-start | bytes 6291456
  39.6 130.7 %all-reduce.5.cloned.1.call-start = ((), (), s32[]{:S(2)}) async-start(), calls=%async_computation.2 | async-start | bytes 4128768 | tf_op jit(solution)/shard_map/psum | solution.py:64
  101.1 4.5 %copy-start.1 = (bf16[192,1792]{1,0:T(8,128)(2,1)S(1)}, bf16[192,1792]{1,0:T(8,128)(2,1)}, u32[]{:S(2)}) copy-start(bf16[192,1792]{1,0:T(8,128)(2,1)} %get-tuple-element.13) | copy-start | bytes 2064388
  101.1 4.5 %copy-start.2 = (bf16[192,1792]{1,0:T(8,128)(2,1)S(1)}, bf16[192,1792]{1,0:T(8,128)(2,1)}, u32[]{:S(2)}) copy-start(bf16[192,1792]{1,0:T(8,128)(2,1)} %get-tuple-element.15) | copy-start | bytes 2064388
  101.1 4.5 %copy-start.3 = (bf16[192,1792]{1,0:T(8,128)(2,1)S(1)}, bf16[192,1792]{1,0:T(8,128)(2,1)}, u32[]{:S(2)}) copy-start(bf16[192,1792]{1,0:T(8,128)(2,1)} %get-tuple-element.14) | copy-start | bytes 2064388
  108.8 99.1 %reduce-scatter.2.cloned.1.call-start = ((), (), s32[]{:S(2)}) async-start(), calls=%async_computation.1 | async-start | bytes 491520 | tf_op jit(solution)/shard_map/reduce_scatter | solution.py:77
  170.3 3.9 %copy-start.4 = (bf16[192,1792]{1,0:T(8,128)(2,1)S(1)}, bf16[192,1792]{1,0:T(8,128)(2,1)}, u32[]{:S(2)}) copy-start(bf16[192,1792]{1,0:T(8,128)(2,1)} %get-tuple-element.10) | copy-start | bytes 2064388
  170.3 3.9 %copy-start.5 = (bf16[192,1792]{1,0:T(8,128)(2,1)S(1)}, bf16[192,1792]{1,0:T(8,128)(2,1)}, u32[]{:S(2)}) copy-start(bf16[192,1792]{1,0:T(8,128)(2,1)} %get-tuple-element.11) | copy-start | bytes 2064388
  174.2 3.1 %copy-start.6 = (bf16[192,1792]{1,0:T(8,128)(2,1)S(1)}, bf16[192,1792]{1,0:T(8,128)(2,1)}, u32[]{:S(2)}) copy-start(bf16[192,1792]{1,0:T(8,128)(2,1)} %get-tuple-element.12) | copy-start | bytes 2064388
  177.4 6.4 %slice-start.2 = ((s8[7340032]{0:T(1024)(128)(4,1)}), s8[4194304]{0:T(1024)(128)(4,1)S(1)}, s32[]{:S(2)}) async-start(s8[7340032]{0:T(1024)(128)(4,1)} %bitcast.2), calls=%async_computation.6 | async-start | bytes 8388608
  177.4 7.7 %slice-start.4 = ((s8[7340032]{0:T(1024)(128)(4,1)}), s8[4194304]{0:T(1024)(128)(4,1)S(1)}, s32[]{:S(2)}) async-start(s8[7340032]{0:T(1024)(128)(4,1)} %bitcast.4), calls=%async_computation.8 | async-start | bytes 8388608
  180.6 3.1 %slice-start.3 = ((s8[7340032]{0:T(1024)(128)(4,1)}), s8[3145728]{0:T(1024)(128)(4,1)S(1)}, s32[]{:S(2)}) async-start(s8[7340032]{0:T(1024)(128)(4,1)} %bitcast.2), calls=%async_computation.7 | async-start | bytes 6291456
  180.6 4.8 %slice-start.5 = ((s8[7340032]{0:T(1024)(128)(4,1)}), s8[3145728]{0:T(1024)(128)(4,1)S(1)}, s32[]{:S(2)}) async-start(s8[7340032]{0:T(1024)(128)(4,1)} %bitcast.4), calls=%async_computation.9 | async-start | bytes 6291456
  183.7 1.7 copy-start.7
  187.6 7.2 %copy-start = (bf16[1024,1792]{1,0:T(8,128)(2,1)S(1)}, bf16[1024,1792]{1,0:T(8,128)(2,1)}, u32[]{:S(2)}) copy-start(bf16[1024,1792]{1,0:T(8,128)(2,1)} %convolution_convert_fusion.5) | copy-start | bytes 11010052
Sparse Core Ops, SparseCore 0:
  39.7 61.3 all-reduce.6
  108.9 61.3 all-reduce.4
  187.7 20.0 reduce-scatter.1
where the time goes:
time: 215 us; the launch traced here: 214 us
  waiting for transfers between devices  106 us (49%)
  matrix products  54.4 us (25%)
  blocking collectives  21.4 us (10%)
  other arithmetic  17.6 us (8%)
  between operations  13.8 us (6%)
    psum x2, waiting for transfers between devices, body(): sums = lax.psum(parts, 'row')  103 us
    all_gather x1, blocking collectives, body(): both_all = lax.all_gather(both, 'col', axis=0, tiled=True)  21.4 us
    dot_general x6, matrix products, contract_last(): lax.dot_general(left, right, (((1,), (1,)), ((), ())), preferred_element_...  18.6 us
    concatenate x1, other arithmetic, body(): jnp.concatenate(acc_gate, axis=1)  9.45 us
    dot_general x2, matrix products, body(): jnp.dot(tok_all, uw, preferred_element_type=jnp.float32)  7.96 us
    dot_general x2, matrix products, body(): jnp.dot(tok_all, gw, preferred_element_type=jnp.float32)  7.7 us
    dot_general x2, matrix products, contract_first(): lax.dot_general(left, right, (((0,), (0,)), ((), ())), preferred_element_...  7.56 us
    concatenate x1, other arithmetic, body(): jnp.concatenate(acc_down, axis=0)  7.2 us
  transfers between devices with their start and end apart: 3, of which 3 were waited for; matrix products, arithmetic and copies ran while one was open for 17% of the time, Pallas kernels for 0%

commit v1 on v0

--- a/solution.py
+++ b/solution.py
@@ -2,6 +2,14 @@
 import jax.numpy as jnp
 from jax import lax
 from jax.sharding import PartitionSpec as P
+from jax.lax import axis_index, ppermute, psum
+
+
+def refer_shards_on_mesh(buf, where_dim):
+    oldest = list(buf.shape[1:])
+    oldest[where_dim] *= buf.shape[0]
+    work_now = jnp.moveaxis(buf, 0, where_dim).reshape(oldest)
+    return work_now
 
 
 def contract_first(left, right):
@@ -39,7 +47,24 @@
 def body(tokens, grad_out, gate_weight, up_weight, down_weight):
     feat = tokens.shape[1]
     both = jnp.concatenate([tokens, grad_out], axis=1)
-    both_all = lax.all_gather(both, "col", axis=0, tiled=True)
+    n_axis = psum(1, "col")
+    gallery = []
+    for m in range(n_axis):
+        gallery.append((m, (m + 1) % n_axis))
+    entries = []
+    for w, no in gallery:
+        entries.append((no, w))
+    item_now, even = ([], [])
+    for k0 in range(n_axis - 1):
+        if k0 % 2 == 0:
+            item_now.append(ppermute(item_now[-1] if item_now else both, "col", gallery))
+        else:
+            even.append(ppermute(even[-1] if even else both, "col", entries))
+    arr_now = jnp.stack([*item_now[::-1], both, *even], axis=0)
+    state_next = axis_index("col")
+    o_now = state_next - len(item_now)
+    arr_now = arr_now[(jnp.arange(n_axis) - o_now) % n_axis]
+    both_all = refer_shards_on_mesh(arr_now, 0)
     tok_all = both_all[:, :feat]
     grad_all = both_all[:, feat:]
     tok_t = tok_all.T

time: 215 us -> 216 us (level)
  blocking collectives: 21.4 us -> 0 us
  waiting for transfers between devices: 106 us -> 120 us
  starting transfers between devices: 0.3 us -> 5.44 us
  local copies, waits for them, and re-layouts: 0.36 us -> 2.74 us
    all_gather x1 -> x0, blocking collectives: 21.4 us -> none  [body(): both_all = lax.all_gather(both, 'col', axis=0, tiled=True)]
    ppermute x0 -> x3, waiting for transfers between devices: none -> 13.7 us  [the longest x2 11 us: body(): ppermute(item_now[-1] if item_now else both, 'col', gallery)]
    ppermute x0 -> x3, starting transfers between devices: none -> 5.14 us  [the longest x2 3.05 us: body(): ppermute(item_now[-1] if item_now else both, 'col', gallery)]
  transfers between devices with their start and end apart: 3 -> 6, of which waited for: 3 -> 6; matrix products, arithmetic and copies ran while one was open for 17% -> 17% of each run, Pallas kernels for 0% -> 0%
where the time goes in v1:
time: 216 us
  waiting for transfers between devices  120 us (56%)
  matrix products  56.2 us (26%)
  other arithmetic  16.8 us (8%)
  between operations  13.8 us (6%)
  starting transfers between devices  5.44 us (3%)
  local copies, waits for them, and re-layouts  2.74 us (1%)
    psum x2, waiting for transfers between devices, body(): sums = lax.psum(parts, 'row')  103 us
    dot_general x6, matrix products, contract_last(): lax.dot_general(left, right, (((1,), (1,)), ((), ())), preferred_element_...  20.6 us
    ppermute x2, waiting for transfers between devices, body(): ppermute(item_now[-1] if item_now else both, 'col', gallery)  11 us
    concatenate x1, other arithmetic, body(): jnp.concatenate(acc_gate, axis=1)  9.45 us
    dot_general x2, matrix products, body(): jnp.dot(tok_all, uw, preferred_element_type=jnp.float32)  7.94 us
    dot_general x2, matrix products, contract_first(): lax.dot_general(left, right, (((0,), (0,)), ((), ())), preferred_element_...  7.59 us
    dot_general x2, matrix products, body(): jnp.dot(tok_all, gw, preferred_element_type=jnp.float32)  7.55 us
    concatenate x1, other arithmetic, body(): jnp.concatenate(acc_down, axis=0)  7.2 us
  transfers between devices with their start and end apart: 6, of which 6 were waited for; matrix products, arithmetic and copies ran while one was open for 17% of the time, Pallas kernels for 0%

profile of v1, /device:TPU:0, one launch (start us, length us, event | category | flops | bytes accessed | tf_op | source)
XLA Modules:
  0.0 215.5 jit_solution(11257819307568805385)
XLA Ops:
  7.2 0.0 all-reduce.7.cloned.1.call-start
  7.2 0.9 constant_dynamic-update-slice_fusion.1
  8.1 0.9 constant_dynamic-update-slice_fusion
  9.0 3.1 %collective-permute-start = (bf16[48,2048]{1,0:T(8,128)(2,1)S(1)}, bf16[48,2048]{1,0:T(8,128)(2,1)S(1)}, u32[]{:S(2)}, u32[]{:S(2)}) collective-permute-start(bf16[48,2048]{1,0:T(8,128)(2,1)S(1)} %constant_dynamic-update-slice_fusion), channel_id=1, source_target_pairs={{0,1},{1,2},{2,3},{3,0},{4,5},{5,6},{6,7},{7,4},{8,9},{9,10},{10,1... | collective-permute-start | bytes 589832 | tf_op jit(solution)/shard_map/ppermute | solution.py:60
  12.1 2.1 collective-permute-start.2
  14.1 5.7 %collective-permute-done = bf16[48,2048]{1,0:T(8,128)(2,1)S(1)} collective-permute-done((bf16[48,2048]{1,0:T(8,128)(2,1)S(1)}, bf16[48,2048]{1,0:T(8,128)(2,1)S(1)}, u32[]{:S(2)}, u32[]{:S(2)}) %collective-permute-start) | collective-permute-done | bytes 196640 | tf_op jit(solution)/shard_map/ppermute | solution.py:60
  19.9 0.0 collective-permute-start.1
  19.9 2.7 %collective-permute-done.2 = bf16[48,2048]{1,0:T(8,128)(2,1)S(1)} collective-permute-done((bf16[48,2048]{1,0:T(8,128)(2,1)S(1)}, bf16[48,2048]{1,0:T(8,128)(2,1)S(1)}, u32[]{:S(2)}, u32[]{:S(2)}) %collective-permute-start.2) | collective-permute-done | bytes 196640 | tf_op jit(solution)/shard_map/ppermute | solution.py:62
  22.6 5.2 %collective-permute-done.1 = bf16[48,2048]{1,0:T(8,128)(2,1)S(1)} collective-permute-done((bf16[48,2048]{1,0:T(8,128)(2,1)S(1)}, bf16[48,2048]{1,0:T(8,128)(2,1)S(1)}, u32[]{:S(2)}, u32[]{:S(2)}) %collective-permute-start.1) | collective-permute-done | bytes 196640 | tf_op jit(solution)/shard_map/ppermute | solution.py:60
  27.9 0.1 pad_maximum_fusion.3
  28.0 0.6 gather_fusion
  28.6 3.8 %fusion.23 = bf16[192,1792]{1,0:T(8,128)(2,1)} fusion(bf16[1024,3584]{1,0:T(8,128)(2,1)} %param.7, bf16[192,2048]{1,0:T(8,128)(2,1)S(1)} %bitcast.7), kind=kOutput, calls=%fused_computation.31 | convolution fusion | flops 704987136 | bytes 4751360 | tf_op jit(solution)/shard_map/dot_general | solution.py:83
  32.4 3.8 %fusion.20 = bf16[192,1792]{1,0:T(8,128)(2,1)} fusion(bf16[1024,3584]{1,0:T(8,128)(2,1)} %param.8, bf16[192,2048]{1,0:T(8,128)(2,1)S(1)} %bitcast.8), kind=kOutput, calls=%fused_computation.30 | convolution fusion | flops 704987136 | bytes 4751360 | tf_op jit(solution)/shard_map/dot_general | solution.py:84
  36.1 4.3 %fusion.32 = bf16[192,1792]{1,0:T(8,128)(2,1)} fusion(bf16[3584,1024]{1,0:T(8,128)(2,1)} %param.9, bf16[192,2048]{1,0:T(8,128)(2,1)S(1)} %bitcast.9), kind=kOutput, calls=%fused_computation.34 | convolution fusion | flops 704987136 | bytes 4751360 | tf_op jit(solution)/shard_map/dot_general | solution.py:22
  40.4 0.0 all-reduce.7.cloned.1.call-update
  40.4 0.0 all-reduce.5.cloned.1.call-start
  40.5 3.8 %fusion.26 = bf16[192,1792]{1,0:T(8,128)(2,1)} fusion(bf16[1024,3584]{1,0:T(8,128)(2,1)} %param.7, bf16[192,2048]{1,0:T(8,128)(2,1)S(1)} %bitcast.10), kind=kOutput, calls=%fused_computation.32 | convolution fusion | flops 704987136 | bytes 4751360 | tf_op jit(solution)/shard_map/dot_general | solution.py:83
  44.2 4.2 %fusion.29 = bf16[192,1792]{1,0:T(8,128)(2,1)} fusion(bf16[1024,3584]{1,0:T(8,128)(2,1)} %param.8, bf16[192,2048]{1,0:T(8,128)(2,1)S(1)} %bitcast.11), kind=kOutput, calls=%fused_computation.33 | convolution fusion | flops 704987136 | bytes 4751360 | tf_op jit(solution)/shard_map/dot_general | solution.py:84
  48.4 4.3 %fusion.35 = bf16[192,1792]{1,0:T(8,128)(2,1)} fusion(bf16[3584,1024]{1,0:T(8,128)(2,1)} %param.9, bf16[192,2048]{1,0:T(8,128)(2,1)S(1)} %bitcast.12), kind=kOutput, calls=%fused_computation.35 | convolution fusion | flops 704987136 | bytes 4751360 | tf_op jit(solution)/shard_map/dot_general | solution.py:22
  52.7 49.6 %all-reduce.7.cloned.1.call-done = (bf16[192,1792]{1,0:T(8,128)(2,1)}, bf16[192,1792]{1,0:T(8,128)(2,1)}, bf16[192,1792]{1,0:T(8,128)(2,1)}) async-done(((bf16[192,1792]{1,0:T(8,128)(2,1)}, bf16[192,1792]{1,0:T(8,128)(2,1)}, bf16[192,1792]{1,0:T(8,128)(2,1)}), (bf16[192,1792]{1,0:T(8,128)(2,1)}, bf16[192,1792]{1,0:T(8,128)(2,1)}, bf16[192,1792]{1,0:T(8,128)(2,1)})) %all-reduce.7.cloned.1.call-update) | async-done | bytes 2064400 | tf_op jit(solution)/shard_map/psum | solution.py:89
  102.3 4.5 %convolution_convert_fusion.1 = bf16[1792,1024]{1,0:T(8,128)(2,1)} fusion(bf16[192,1792]{1,0:T(8,128)(2,1)} %get-tuple-element.14, bf16[192,1792]{1,0:T(8,128)(2,1)} %get-tuple-element.13, bf16[192,2048]{1,0:T(8,128)(2,1)S(1)} %bitcast.13), kind=kOutput, calls=%fused_computation.5 | convolution fusion | flops 709230592 | bytes 5439488 | tf_op jit(solution)/shard_map/dot_general | solution.py:16
  106.8 0.0 copy-done.1
  106.8 0.0 copy-done.2
  106.8 0.0 copy-done.3
  106.8 3.2 %convolution_convert_fusion.5 = bf16[1024,1792]{1,0:T(8,128)(2,1)} fusion(bf16[192,2048]{1,0:T(8,128)(2,1)S(1)} %bitcast.14, bf16[192,1792]{1,0:T(8,128)(2,1)S(1)} %copy-done.3, bf16[192,1792]{1,0:T(8,128)(2,1)S(1)} %copy-done.2, bf16[192,1792]{1,0:T(8,128)(2,1)S(1)} %copy-done.1), kind=kOutput, calls=%fused_computation.9 | convolution fusion | flops 710950912 | bytes 6127616 | tf_op jit(solution)/shard_map/dot_general | solution.py:94
  109.9 0.0 all-reduce.5.cloned.1.call-update
  109.9 0.2 reduce-scatter.2.cloned.1.call-start
  110.2 3.0 %convolution_convert_fusion.3 = bf16[1024,1792]{1,0:T(8,128)(2,1)} fusion(bf16[192,2048]{1,0:T(8,128)(2,1)S(1)} %bitcast.15, bf16[192,1792]{1,0:T(8,128)(2,1)S(1)} %copy-done.1, bf16[192,1792]{1,0:T(8,128)(2,1)S(1)} %copy-done.2), kind=kOutput, calls=%fused_computation.7 | convolution fusion | flops 709230592 | bytes 5439488 | tf_op jit(solution)/shard_map/dot_general | solution.py:97
  113.2 4.6 %fusion.12 = f32[192,1024]{1,0:T(8,128)} fusion(bf16[1024,3584]{1,0:T(8,128)(2,1)} %param.7, bf16[192,1792]{1,0:T(8,128)(2,1)S(1)} %copy-done.3, bf16[192,1792]{1,0:T(8,128)(2,1)S(1)} %copy-done.2, bf16[192,1792]{1,0:T(8,128)(2,1)S(1)} %copy-done.1), kind=kOutput, calls=%fused_computation.22 | convolution fusion | flops 709115904 | bytes 6520832 | tf_op jit(solution)/shard_map/dot_general | solution.py:22
  117.8 53.6 %all-reduce.5.cloned.1.call-done = (bf16[192,1792]{1,0:T(8,128)(2,1)}, bf16[192,1792]{1,0:T(8,128)(2,1)}, bf16[192,1792]{1,0:T(8,128)(2,1)}) async-done(((bf16[192,1792]{1,0:T(8,128)(2,1)}, bf16[192,1792]{1,0:T(8,128)(2,1)}, bf16[192,1792]{1,0:T(8,128)(2,1)}), (bf16[192,1792]{1,0:T(8,128)(2,1)}, bf16[192,1792]{1,0:T(8,128)(2,1)}, bf16[192,1792]{1,0:T(8,128)(2,1)})) %all-reduce.5.cloned.1.call-update) | async-done | bytes 2064400 | tf_op jit(solution)/shard_map/psum | solution.py:89
  171.5 3.9 %fusion.4 = f32[192,1024]{1,0:T(8,128)S(1)} fusion(bf16[1024,3584]{1,0:T(8,128)(2,1)} %param.8, bf16[192,1792]{1,0:T(8,128)(2,1)} %get-tuple-element.10, bf16[192,1792]{1,0:T(8,128)(2,1)} %get-tuple-element.11), kind=kOutput, calls=%fused_computation.14 | convolution fusion | flops 707395584 | bytes 5832704 | tf_op jit(solution)/shard_map/dot_general | solution.py:22
  175.4 0.0 copy-done.4
  175.4 0.0 copy-done.5
  175.4 3.1 %convolution_convert_fusion.2 = bf16[1024,1792]{1,0:T(8,128)(2,1)} fusion(bf16[192,2048]{1,0:T(8,128)(2,1)S(1)} %bitcast.16, bf16[192,1792]{1,0:T(8,128)(2,1)S(1)} %copy-done.4, bf16[192,1792]{1,0:T(8,128)(2,1)S(1)} %copy-done.5), kind=kOutput, calls=%fused_computation.6 | convolution fusion | flops 709230592 | bytes 5439488 | tf_op jit(solution)/shard_map/dot_general | solution.py:97
  178.5 0.0 copy-done.6
  178.5 3.2 %convolution_convert_fusion.4 = bf16[1024,1792]{1,0:T(8,128)(2,1)} fusion(bf16[192,2048]{1,0:T(8,128)(2,1)S(1)} %bitcast.17, bf16[192,1792]{1,0:T(8,128)(2,1)S(1)} %copy-done.6, bf16[192,1792]{1,0:T(8,128)(2,1)S(1)} %copy-done.5, bf16[192,1792]{1,0:T(8,128)(2,1)S(1)} %copy-done.4), kind=kOutput, calls=%fused_computation.8 | convolution fusion | flops 710950912 | bytes 6127616 | tf_op jit(solution)/shard_map/dot_general | solution.py:94
  181.8 3.1 %convolution_convert_fusion = bf16[1792,1024]{1,0:T(8,128)(2,1)} fusion(bf16[192,1792]{1,0:T(8,128)(2,1)S(1)} %copy-done.6, bf16[192,1792]{1,0:T(8,128)(2,1)S(1)} %copy-done.4, bf16[192,2048]{1,0:T(8,128)(2,1)S(1)} %bitcast.18), kind=kOutput, calls=%fused_computation.4 | convolution fusion | flops 709230592 | bytes 5439488 | tf_op jit(solution)/shard_map/dot_general | solution.py:16
  184.9 1.4 fusion.64
  186.3 0.0 slice-done.2
  186.3 0.3 slice-done.3
  186.6 0.0 copy-done.7
  186.6 2.2 %fusion.67 = bf16[192,1024]{1,0:T(8,128)(2,1)} fusion(f32[192,1024]{1,0:T(8,128)S(1)} %fusion.64, f32[192,1024]{1,0:T(8,128)S(1)} %copy-done.7, bf16[1024,3584]{1,0:T(8,128)(2,1)S(1)} %bitcast.26, bf16[192,1792]{1,0:T(8,128)(2,1)S(1)} %copy-done.1, bf16[192,1792]{1,0:T(8,128)(2,1)S(1)} %copy-done.2), kind=kOutput, calls=%fused_computation.71 | convolution fusion | flops 707985408 | bytes 7012352 | tf_op jit(solution)/shard_map/dot_general | solution.py:22
  188.7 0.0 reduce-scatter.2.cloned.1.call-update
  188.8 0.0 copy-start
  188.8 7.2 %pad_maximum_fusion.2 = bf16[3584,1024]{1,0:T(8,128)(2,1)} fusion(bf16[1792,1024]{1,0:T(8,128)(2,1)} %convolution_convert_fusion, bf16[1792,1024]{1,0:T(8,128)(2,1)} %convolution_convert_fusion.1), kind=kLoop, calls=%fused_computation.3 | loop fusion | flops 14680064 | bytes 14680064 | tf_op jit(solution)/shard_map/concatenate | solution.py:109
  196.0 0.0 copy-done
  196.0 9.5 %pad_maximum_fusion = (bf16[1024,3584]{1,0:T(8,128)(2,1)}, bf16[1024,3584]{1,0:T(8,128)(2,1)}) fusion(bf16[1024,1792]{1,0:T(8,128)(2,1)} %convolution_convert_fusion.4, bf16[1024,1792]{1,0:T(8,128)(2,1)S(1)} %copy-done, bf16[1024,1792]{1,0:T(8,128)(2,1)} %convolution_convert_fusion.2, bf16[1024,1792]{1,0:T(8,128)(2,1)} %convolution_convert_fusion.3), kind=kLoop, calls=%fused_computation.1 | loop fusion | flops 29360128 | bytes 29360128 | tf_op jit(solution)/shard_map/concatenate | solution.py:107
  205.4 3.5 %reduce-scatter.2.cloned.1.call-done = bf16[48,1024]{1,0:T(8,128)(2,1)} async-done(((bf16[192,1024]{1,0:T(8,128)(2,1)}), bf16[48,1024]{1,0:T(8,128)(2,1)}) %reduce-scatter.2.cloned.1.call-update) | async-done | bytes 98320 | tf_op jit(solution)/shard_map/reduce_scatter | solution.py:102
  (17 shorter events, 0.0 us)
Async XLA Ops:
  7.2 95.1 %all-reduce.7.cloned.1.call-start = ((), (), s32[]{:S(2)}) async-start(), calls=%async_computation.3 | async-start | bytes 4128768 | tf_op jit(solution)/shard_map/psum | solution.py:89
  9.0 10.9 %collective-permute-start = (bf16[48,2048]{1,0:T(8,128)(2,1)S(1)}, bf16[48,2048]{1,0:T(8,128)(2,1)S(1)}, u32[]{:S(2)}, u32[]{:S(2)}) collective-permute-start(bf16[48,2048]{1,0:T(8,128)(2,1)S(1)} %constant_dynamic-update-slice_fusion), channel_id=1, source_target_pairs={{0,1},{1,2},{2,3},{3,0},{4,5},{5,6},{6,7},{7,4},{8,9},{9,10},{10,1... | collective-permute-start | bytes 589832 | tf_op jit(solution)/shard_map/ppermute | solution.py:60
  12.1 10.6 %collective-permute-start.2 = (bf16[48,2048]{1,0:T(8,128)(2,1)S(1)}, bf16[48,2048]{1,0:T(8,128)(2,1)S(1)}, u32[]{:S(2)}, u32[]{:S(2)}) collective-permute-start(bf16[48,2048]{1,0:T(8,128)(2,1)S(1)} %constant_dynamic-update-slice_fusion), channel_id=1, source_target_pairs={{1,0},{2,1},{3,2},{0,3},{5,4},{6,5},{7,6},{4,7},{9,8},{10,9},{11,1... | collective-permute-start | bytes 589832 | tf_op jit(solution)/shard_map/ppermute | solution.py:62
  19.9 8.0 %collective-permute-start.1 = (bf16[48,2048]{1,0:T(8,128)(2,1)S(1)}, bf16[48,2048]{1,0:T(8,128)(2,1)S(1)}, u32[]{:S(2)}, u32[]{:S(2)}) collective-permute-start(bf16[48,2048]{1,0:T(8,128)(2,1)S(1)} %collective-permute-done), channel_id=1, source_target_pairs={{0,1},{1,2},{2,3},{3,0},{4,5},{5,6},{6,7},{7,4},{8,9},{9,10},{10,1... | collective-permute-start | bytes 589832 | tf_op jit(solution)/shard_map/ppermute | solution.py:60
  40.4 131.0 %all-reduce.5.cloned.1.call-start = ((), (), s32[]{:S(2)}) async-start(), calls=%async_computation.2 | async-start | bytes 4128768 | tf_op jit(solution)/shard_map/psum | solution.py:89
  102.3 4.5 %copy-start.1 = (bf16[192,1792]{1,0:T(8,128)(2,1)S(1)}, bf16[192,1792]{1,0:T(8,128)(2,1)}, u32[]{:S(2)}) copy-start(bf16[192,1792]{1,0:T(8,128)(2,1)} %get-tuple-element.13) | copy-start | bytes 2064388
  102.3 4.5 %copy-start.2 = (bf16[192,1792]{1,0:T(8,128)(2,1)S(1)}, bf16[192,1792]{1,0:T(8,128)(2,1)}, u32[]{:S(2)}) copy-start(bf16[192,1792]{1,0:T(8,128)(2,1)} %get-tuple-element.15) | copy-start | bytes 2064388
  102.3 4.5 %copy-start.3 = (bf16[192,1792]{1,0:T(8,128)(2,1)S(1)}, bf16[192,1792]{1,0:T(8,128)(2,1)}, u32[]{:S(2)}) copy-start(bf16[192,1792]{1,0:T(8,128)(2,1)} %get-tuple-element.14) | copy-start | bytes 2064388
  109.9 99.0 %reduce-scatter.2.cloned.1.call-start = ((), (), s32[]{:S(2)}) async-start(), calls=%async_computation.1 | async-start | bytes 491520 | tf_op jit(solution)/shard_map/reduce_scatter | solution.py:102
  171.5 3.9 %copy-start.4 = (bf16[192,1792]{1,0:T(8,128)(2,1)S(1)}, bf16[192,1792]{1,0:T(8,128)(2,1)}, u32[]{:S(2)}) copy-start(bf16[192,1792]{1,0:T(8,128)(2,1)} %get-tuple-element.10) | copy-start | bytes 2064388
  171.5 3.9 %copy-start.5 = (bf16[192,1792]{1,0:T(8,128)(2,1)S(1)}, bf16[192,1792]{1,0:T(8,128)(2,1)}, u32[]{:S(2)}) copy-start(bf16[192,1792]{1,0:T(8,128)(2,1)} %get-tuple-element.11) | copy-start | bytes 2064388
  175.4 3.1 %copy-start.6 = (bf16[192,1792]{1,0:T(8,128)(2,1)S(1)}, bf16[192,1792]{1,0:T(8,128)(2,1)}, u32[]{:S(2)}) copy-start(bf16[192,1792]{1,0:T(8,128)(2,1)} %get-tuple-element.12) | copy-start | bytes 2064388
  178.5 6.4 %slice-start = ((s8[7340032]{0:T(1024)(128)(4,1)}), s8[4194304]{0:T(1024)(128)(4,1)S(1)}, s32[]{:S(2)}) async-start(s8[7340032]{0:T(1024)(128)(4,1)} %bitcast.23), calls=%async_computation.4 | async-start | bytes 8388608
  178.5 7.7 %slice-start.2 = ((s8[7340032]{0:T(1024)(128)(4,1)}), s8[4194304]{0:T(1024)(128)(4,1)S(1)}, s32[]{:S(2)}) async-start(s8[7340032]{0:T(1024)(128)(4,1)} %bitcast.25), calls=%async_computation.6 | async-start | bytes 8388608
  181.8 3.1 %slice-start.1 = ((s8[7340032]{0:T(1024)(128)(4,1)}), s8[3145728]{0:T(1024)(128)(4,1)S(1)}, s32[]{:S(2)}) async-start(s8[7340032]{0:T(1024)(128)(4,1)} %bitcast.23), calls=%async_computation.5 | async-start | bytes 6291456
  181.8 4.8 %slice-start.3 = ((s8[7340032]{0:T(1024)(128)(4,1)}), s8[3145728]{0:T(1024)(128)(4,1)S(1)}, s32[]{:S(2)}) async-start(s8[7340032]{0:T(1024)(128)(4,1)} %bitcast.25), calls=%async_computation.7 | async-start | bytes 6291456
  184.9 1.7 copy-start.7
  188.8 7.2 %copy-start = (bf16[1024,1792]{1,0:T(8,128)(2,1)S(1)}, bf16[1024,1792]{1,0:T(8,128)(2,1)}, u32[]{:S(2)}) copy-start(bf16[1024,1792]{1,0:T(8,128)(2,1)} %convolution_convert_fusion.5) | copy-start | bytes 11010052
Sparse Core Ops, SparseCore 0:
  40.5 61.6 all-reduce.6
  110.1 61.3 all-reduce.4
  188.9 20.0 reduce-scatter.1
